TPU v7x, 32 devices: a whole 2x2x4 slice. The times are simulated.
32 devices in a mesh: req: 8 (over y, x, core), head: 4 (over z).
Axes of the slice: x: 2, y: 2, z: 4, core: 2. Of those that a mesh axis runs over, the one named last changes fastest.
Arguments:
- tokens: bfloat16 [4096, 2048], P('req'), may hold values from -6 to 6
- norm_gain: float32 [2048], replicated, may hold values from 0.1 to 1.9
- router_weight: float32 [2048, 8], replicated, may hold values from -0.125 to 0.125
- kv_weight: bfloat16 [2048, 4096], P('req', 'head'), may hold values from -0.125 to 0.125
- query_weight: bfloat16 [8, 2048, 2048], P(None, 'req', 'head'), may hold values from -0.125 to 0.125
- out_weight: bfloat16 [8, 2048, 2048], P(None, 'head', 'req'), may hold values from -0.5 to 0.5
- expert_ids: int32 [4096, 2], P('req'), may hold values from 0 to 7, all different within a row
- lengths: int32 [8], replicated, may hold values from 128 to 2048, as said below
- kv_cache: bfloat16 [8, 16, 2048, 256], P('req', 'head'), may hold values from -320 to 320
Outputs:
- attended: bfloat16 [4096, 2048], P(('req', 'head'))
- new_kv: bfloat16 [8, 16, 512, 256], P('req', 'head')
Inputs may be any that keep to these rules, and one draw needn't show every extreme that they name: `lengths`: some request holds exactly 2048 cached positions.
All inputs are finite; a program needn't handle non-finite values.
Results may differ from a plain program's by a relative error of at most 0.012.
The roundings to bfloat16 on the way count: a program that leaves them out, or rounds other values in their place, can miss the bound.
Values may be sent and summed in bfloat16 or wider, within the bound.
No kernel may reach another device: no remote copies, remote signals or barrier semaphores. Data moves between devices by JAX's collectives and lax.ppermute only.
A program may use at most 128 MiB of HBM per device.

v0:
```python
import math
import jax
import jax.numpy as jnp
from jax import lax
from jax.sharding import PartitionSpec as P

NEG_LARGE = -1e30
EPSILON = 1e-06


def normalize(tokens, norm_gain):
    widened = tokens.astype(jnp.float32)
    factor = lax.rsqrt(jnp.mean(widened * widened, axis=-1, keepdims=True) + EPSILON)
    return (widened * factor * norm_gain).astype(jnp.bfloat16)


def gate_pair(normed, router_weight, expert_ids):
    logits = jnp.dot(normed.astype(jnp.float32), router_weight, precision=lax.Precision.HIGHEST)
    one_hot = jnp.arange(router_weight.shape[1])[None, None, :] == expert_ids[:, :, None]
    chosen = jnp.sum(jnp.where(one_hot, logits[:, None, :], 0.0), axis=-1)
    logit_gap = chosen[:, 1] - chosen[:, 0]
    return jnp.stack([1.0 / (1.0 + jnp.exp(logit_gap)), 1.0 / (1.0 + jnp.exp(-logit_gap))], axis=1)


def rotate(vectors, positions):
    half_dim = vectors.shape[-1] // 2
    inv_freq = jnp.exp(-math.log(10000.0) * jnp.arange(half_dim, dtype=jnp.float32) / half_dim)
    angles = positions[:, None] * inv_freq[None, :]
    cosine_table = jnp.cos(angles)
    sine_table = jnp.sin(angles)
    front_half = vectors[..., :half_dim]
    back_half = vectors[..., half_dim:]
    return jnp.concatenate(
        [
            front_half * cosine_table - back_half * sine_table,
            back_half * cosine_table + front_half * sine_table,
        ],
        axis=-1,
    )


def pick_length(lengths, wanted):
    return jnp.sum(jnp.where(jnp.arange(lengths.shape[0]) == wanted, lengths, 0))


def absorb(carry_state, queries, key_rows, value_rows, allowed):
    row_peak, row_total, row_accum = carry_state
    scale_factor = queries.shape[-1] ** (-0.5)
    scores = (
        jnp.einsum("hqd,hkd->hqk", queries, key_rows, preferred_element_type=jnp.float32)
        * scale_factor
    )
    scores = jnp.where(allowed[None], scores, NEG_LARGE)
    new_peak = jnp.maximum(row_peak, jnp.max(scores, axis=-1))
    weights = jnp.where(allowed[None], jnp.exp(scores - new_peak[..., None]), 0.0)
    shrink = jnp.exp(row_peak - new_peak)
    row_total = row_total * shrink + jnp.sum(weights, axis=-1)
    row_accum = row_accum * shrink[..., None] + jnp.einsum(
        "hqk,hkd->hqd", weights.astype(jnp.bfloat16), value_rows, preferred_element_type=jnp.float32
    )
    return (new_peak, row_total, row_accum)


def cache_pass(
    queries, source, lowest, highest, first_block, last_block, anchor, block_len, carry_state
):
    head_dim = source.shape[2] // 2

    def block_step(block_id, running):
        block_rows = lax.dynamic_slice_in_dim(source, block_id * block_len, block_len, 1)
        key_index = anchor + block_id * block_len + jnp.arange(block_len)
        allowed = ((key_index >= lowest) & (key_index < highest))[None, :]
        return absorb(
            running, queries, block_rows[..., :head_dim], block_rows[..., head_dim:], allowed
        )

    return lax.fori_loop(
        jnp.asarray(first_block, jnp.int32),
        jnp.asarray(last_block, jnp.int32),
        block_step,
        carry_state,
    )


def chain_reduce(parts, axis):
    count = lax.axis_size(axis)
    me = lax.axis_index(axis)
    blocks = parts.reshape(count, parts.shape[0] // count, parts.shape[1])
    own = lax.dynamic_index_in_dim(blocks, me, 0, keepdims=False).astype(jnp.float32)
    if count == 1:
        return own.astype(parts.dtype)

    def run(step_block, pairs_of):
        received = None
        for step in range(1, count):
            block = lax.dynamic_index_in_dim(
                blocks, jnp.clip(step_block(step), 0, count - 1), 0, keepdims=False
            )
            if received is not None:
                block = (received.astype(jnp.float32) + block.astype(jnp.float32)).astype(
                    parts.dtype
                )
            received = lax.ppermute(block, axis, pairs_of(step))
        return received.astype(jnp.float32)

    rightward = run(
        lambda step: me + count - step,
        lambda step: [(src, src + 1) for src in range(step) if src + 1 < count],
    )
    leftward = run(
        lambda step: me - count + step,
        lambda step: [(src, src - 1) for src in range(count - step, count) if src >= 1],
    )
    return (own + rightward + leftward).astype(parts.dtype)


def exchange_reduce(rows, weight, axis):
    count = lax.axis_size(axis)
    me = lax.axis_index(axis)
    span = rows.shape[0] // count
    total = None
    for shift in list(range(1, count)) + [0]:
        target = lax.rem(me + shift, count)
        block_rows = lax.dynamic_slice_in_dim(rows, target * span, span, 0)
        part = jnp.dot(block_rows, weight, preferred_element_type=jnp.float32).astype(jnp.bfloat16)
        if shift:
            part = lax.ppermute(part, axis, [(src, (src + shift) % count) for src in range(count)])
        part = part.astype(jnp.float32)
        total = part if total is None else total + part
    return total.astype(jnp.bfloat16)


def shards(
    tokens,
    norm_gain,
    router_weight,
    kv_weight,
    query_weight,
    out_weight,
    expert_ids,
    lengths,
    kv_cache,
):
    normed = normalize(tokens, norm_gain)
    tok_count = normed.shape[0]
    experts = query_weight.shape[0]
    head_dim = kv_cache.shape[3] // 2
    local_heads = query_weight.shape[2] // head_dim
    cache_len = kv_cache.shape[2]
    block_len = min(512, cache_len // 4)
    gate_values = gate_pair(normed, router_weight, expert_ids)
    query_full = lax.all_gather(query_weight, "req", axis=1, tiled=True)
    query_full, kv_weight, out_weight = lax.optimization_barrier(
        (query_full, kv_weight, out_weight)
    )
    kv_full = lax.all_gather(kv_weight, "req", axis=0, tiled=True)
    out_full = lax.all_gather(out_weight, "req", axis=2, tiled=True)
    projected = jnp.dot(normed, kv_full, preferred_element_type=jnp.float32)
    query_all = jnp.einsum("tc,ecn->ten", normed, query_full, preferred_element_type=jnp.float32)
    req_index = lax.axis_index("req")
    own_length = pick_length(lengths, req_index)
    positions = (own_length + jnp.arange(tok_count)).astype(jnp.float32)
    projected = projected.reshape(tok_count, local_heads, 2, head_dim)
    new_keys = rotate(jnp.transpose(projected[:, :, 0], (1, 0, 2)), positions)
    new_values = jnp.transpose(projected[:, :, 1], (1, 0, 2))
    fresh_kv = jnp.concatenate([new_keys, new_values], axis=-1).astype(jnp.bfloat16)
    one_hot = jnp.arange(experts)[None, None, :] == expert_ids[:, :, None]
    query_sel = jnp.sum(jnp.where(one_hot[..., None], query_all[:, None], 0.0), axis=2)
    queries = jnp.transpose(query_sel.reshape(tok_count * 2, local_heads, head_dim), (1, 0, 2))
    queries = rotate(queries, jnp.repeat(positions, 2)).astype(jnp.bfloat16)
    own_cache = kv_cache[0]
    query_rows = tok_count * 2
    empty_state = (
        jnp.full((local_heads, query_rows), NEG_LARGE, jnp.float32),
        jnp.zeros((local_heads, query_rows), jnp.float32),
        jnp.zeros((local_heads, query_rows, head_dim), jnp.float32),
    )
    carry_state = cache_pass(
        queries,
        own_cache,
        0,
        own_length,
        0,
        (own_length + block_len - 1) // block_len,
        0,
        block_len,
        empty_state,
    )
    row_ids = jnp.arange(query_rows) // 2
    causal = row_ids[:, None] >= jnp.arange(tok_count)[None, :]
    carry_state = absorb(
        carry_state, queries, fresh_kv[..., :head_dim], fresh_kv[..., head_dim:], causal
    )
    heads_out = carry_state[2] / carry_state[1][..., None]
    heads_out = jnp.transpose(heads_out, (1, 0, 2)).reshape(tok_count, 2, local_heads * head_dim)
    weighted = (gate_values[:, :, None] * heads_out).astype(jnp.bfloat16)
    mixture = jnp.sum(jnp.where(one_hot[..., None], weighted[:, :, None, :], 0), axis=1)
    mixture_flat = mixture.reshape(tok_count, experts * local_heads * head_dim)
    flat_piece = out_full.reshape(experts * local_heads * head_dim, out_full.shape[2])
    result = exchange_reduce(mixture_flat, flat_piece, "head")
    return (result, fresh_kv[None])


def solution(mesh):
    placed = (
        P("req", None),
        P(),
        P(),
        P("req", "head"),
        P(None, "req", "head"),
        P(None, "head", "req"),
        P("req", None),
        P(),
        P("req", "head", None, None),
    )
    return jax.shard_map(
        shards,
        mesh=mesh,
        in_specs=placed,
        out_specs=(P(("req", "head"), None), P("req", "head", None, None)),
        check_vma=False,
    )
```

profile of v0, /device:TPU:9, one launch (start us, length us, event | category | flops | bytes accessed | tf_op | source)
XLA Modules:
  0.0 309.7 jit_solution(12866438923315046674)
XLA Ops:
  8.0 93.4 %all-gather.4.cloned.1.call-done = bf16[8,2048,512]{2,1,0:T(8,128)(2,1)} async-done(((bf16[8,256,512]{2,1,0:T(8,128)(2,1)}), bf16[8,2048,512]{2,1,0:T(8,128)(2,1)}) %all-gather.4.cloned.1.call-update) | async-done | bytes 16777232 | tf_op jit(solution)/shard_map/all_gather | solution.py:152
  113.4 11.9 %fusion.31 = f32[512,8,512]{2,0,1:T(8,128)S(1)} fusion(bf16[8,2048,512]{2,1,0:T(8,128)(2,1)} %all-gather.4.cloned.1.call-done, bf16[512,2048]{1,0:T(8,128)(2,1)S(1)} %copy-done.8, f32[2048]{0:T(1024)S(1)} %copy-done.14, f32[512]{0:T(512)S(1)} %add_rsqrt_fusion), kind=kOutput, calls=%fused_computation.44 | convolution fusion | flops 8594128896 | bytes 27273216 | tf_op jit(solution)/shard_map/tc,ecn->ten/dot_general | solution.py:159
  125.2 4.9 %copy.40 = f32[512,8,512]{2,1,0:T(8,128)S(1)} copy(f32[512,8,512]{2,0,1:T(8,128)S(1)} %fusion.31) | data formatting | bytes 16777216 | tf_op jit(solution)/shard_map/tc,ecn->ten/dot_general | solution.py:159
  130.1 8.2 %select_reduce_fusion = f32[512,2,512]{2,1,0:T(2,128)} fusion(f32[512,8,512]{2,1,0:T(8,128)S(1)} %copy.40, pred[512,2,8]{2,1,0:T(4,128)(4,1)S(1)} %copy.38), kind=kLoop, calls=%fused_computation.25 | loop fusion | flops 7864320 | bytes 10493952 | tf_op jit(solution)/shard_map/reduce_sum | solution.py:168
  138.3 3.4 %reshape.253 = f32[1024,4,128]{2,1,0:T(4,128)S(1)} reshape(f32[512,2,512]{2,1,0:T(2,128)} %select_reduce_fusion) | data formatting | bytes 4194304 | tf_op jit(solution)/shard_map/reshape | solution.py:169
  144.7 31.4 %while.14 = (s32[]{:T(128)}, f32[4,1024]{1,0:T(4,128)S(1)}, f32[4,1024]{1,0:T(4,128)S(1)}, f32[4,1024,128]{2,1,0:T(8,128)}, s32[]{:T(128)}, /*index=5*/s32[]{:T(...) while((s32[]{:T(128)}, f32[4,1024]{1,0:T(4,128)S(1)}, ...), condition=%wide.region_7.8_spmd, body=%wide.region_4.7_spmd.sunk | while | flops 1102063616 | bytes 65276644 | solution.py:77
  148.0 2.5 fusion.82
  152.2 9.0 %multiply_add_fusion.6 = f32[4,1024,128]{2,1,0:T(8,128)} fusion(f32[4,1024,128]{2,1,0:T(8,128)} %get-tuple-element.164, f32[4,512,1024]{2,1,0:T(8,128)} %copy-done.2, f32[4,1024]{1,0:T(4,128)S(1)} %max.8, pred[512]{0:T(512)(128)(4,1)S(1)} %fusion.81, f32[4,1024]{1,0:T(4,128)S(1)} %get-tuple-element.147, ...), kind=kOutput, calls=%fused_computation.10.clone.1 | convolution fusion | flops 548405248 | bytes 13141000 | tf_op jit(solution)/shard_map/while/body/hqk,hkd->hqd/dot_general | solution.py:58
  164.3 2.5 fusion.82
  167.5 8.5 %multiply_add_fusion.6 = f32[4,1024,128]{2,1,0:T(8,128)} fusion(f32[4,1024,128]{2,1,0:T(8,128)} %get-tuple-element.164, f32[4,512,1024]{2,1,0:T(8,128)} %copy-done.2, f32[4,1024]{1,0:T(4,128)S(1)} %max.8, pred[512]{0:T(512)(128)(4,1)S(1)} %fusion.81, f32[4,1024]{1,0:T(4,128)S(1)} %get-tuple-element.147, ...), kind=kOutput, calls=%fused_computation.10.clone.1 | convolution fusion | flops 548405248 | bytes 13141000 | tf_op jit(solution)/shard_map/while/body/hqk,hkd->hqd/dot_general | solution.py:58
  176.1 5.9 %fusion.59 = f32[512,1024]{1,0:T(8,128)} fusion(bf16[2048,1024]{1,0:T(8,128)(2,1)} %all-gather.6.cloned.1.call-done, bf16[512,2048]{1,0:T(8,128)(2,1)S(1)} %copy-done.9, f32[2048]{0:T(1024)S(1)} %copy-done.14, f32[512]{0:T(512)S(1)} %add_rsqrt_fusion), kind=kOutput, calls=%fused_computation.101 | convolution fusion | flops 2151677952 | bytes 8398848 | tf_op jit(solution)/shard_map/dot_general | solution.py:158
  181.9 3.7 %reshape.254 = f32[512,4,2,128]{3,2,1,0:T(2,128)S(1)} reshape(f32[512,1024]{1,0:T(8,128)} %fusion.59) | data formatting | bytes 4194304 | tf_op jit(solution)/shard_map/reshape | solution.py:163
  192.2 4.0 %divide_bitcast_fusion = f32[1024,4,128]{2,0,1:T(8,128)S(1)} fusion(f32[4,1024,128]{2,1,0:T(8,128)S(1)} %copy-done.10, f32[4,1024,512]{1,2,0:T(8,128)S(1)} %get-tuple-element.89, f32[4,1024]{1,0:T(4,128)S(1)} %max.6, pred[1024,512]{0,1:T(8,128)(4,1)S(1)} %copy-done.5, f32[4,1024]{1,0:T(4,128)S(1)} %get-tuple-element.76, ...), kind=kOutput, calls=%fused_computation.48 | convolution fusion | flops 548929536 | bytes 13680640 | tf_op jit(solution)/shard_map/hqk,hkd->hqd/dot_general | solution.py:58
  196.2 2.7 copy.45
  198.9 3.0 reshape.255
  203.7 7.2 %select_reduce_fusion.1 = bf16[512,8,512]{2,1,0:T(8,128)(2,1)S(1)} fusion(pred[512,2,8]{2,1,0:T(4,128)(4,1)S(1)} %copy.38, bf16[512,2,512]{2,1,0:T(2,128)(2,1)S(1)} %multiply_convert_fusion), kind=kLoop, calls=%fused_computation.26 | loop fusion | flops 6291456 | bytes 5251072 | tf_op jit(solution)/shard_map/reduce_sum | solution.py:197
  210.9 4.2 %copy.50 = bf16[64,8,8,512]{3,1,2,0:T(8,128)(2,1)} copy(bf16[64,8,8,512]{3,2,1,0:T(8,128)(2,1)S(1)} %bitcast.64) | data formatting | bytes 8388608
  215.1 20.0 %all-gather.8.cloned.1.call-done = bf16[8,512,2048]{2,1,0:T(8,128)(2,1)} async-done(((bf16[8,512,256]{2,1,0:T(8,128)(2,1)}), bf16[8,512,2048]{2,1,0:T(8,128)(2,1)}) %all-gather.8.cloned.1.call-update) | async-done | bytes 16777232 | tf_op jit(solution)/shard_map/all_gather | solution.py:157
  235.1 9.4 %convolution_convert_fusion.3 = bf16[128,2048]{1,0:T(8,128)(2,1)} fusion(bf16[4096,2048]{1,0:T(8,128)(2,1)} %bitcast.59, bf16[512,4096]{1,0:T(8,128)(2,1)} %bitcast.65, s32[]{:T(128)S(6)} %select_n.72), kind=kOutput, calls=%fused_computation.43 | convolution fusion | flops 2147745792 | bytes 18350084 | tf_op jit(solution)/shard_map/dot_general | solution.py:125
  247.4 3.3 %convolution_convert_fusion.2 = bf16[128,2048]{1,0:T(8,128)(2,1)} fusion(bf16[4096,2048]{1,0:T(8,128)(2,1)S(1)} %bitcast.61, bf16[512,4096]{1,0:T(8,128)(2,1)S(1)} %bitcast.67, s32[]{:T(128)S(6)} %select_n.73), kind=kOutput, calls=%fused_computation.42 | convolution fusion | flops 2147745792 | bytes 18350084 | tf_op jit(solution)/shard_map/dot_general | solution.py:125
  252.8 3.3 %convolution_convert_fusion.1 = bf16[128,2048]{1,0:T(8,128)(2,1)} fusion(bf16[4096,2048]{1,0:T(8,128)(2,1)S(1)} %bitcast.62, bf16[512,4096]{1,0:T(8,128)(2,1)S(1)} %bitcast.68, s32[]{:T(128)S(6)} %select_n.74), kind=kOutput, calls=%fused_computation.41 | convolution fusion | flops 2147745792 | bytes 18350084 | tf_op jit(solution)/shard_map/dot_general | solution.py:125
  258.2 32.8 %collective-permute-done.1 = bf16[128,2048]{1,0:T(8,128)(2,1)} collective-permute-done((bf16[128,2048]{1,0:T(8,128)(2,1)}, bf16[128,2048]{1,0:T(8,128)(2,1)}, u32[]{:S(2)}, u32[]{:S(2)}) %collective-permute-start.1) | collective-permute-done | bytes 524320 | tf_op jit(solution)/shard_map/ppermute | solution.py:127
  291.0 2.5 collective-permute-done.2
  293.5 9.5 %add_convert_fusion.1 = bf16[128,2048]{1,0:T(8,128)(2,1)} fusion(bf16[128,2048]{1,0:T(8,128)(2,1)} %collective-permute-done.2, bf16[128,2048]{1,0:T(8,128)(2,1)} %collective-permute-done.1, bf16[128,2048]{1,0:T(8,128)(2,1)S(1)} %collective-permute-done, bf16[4096,2048]{1,0:T(8,128)(2,1)} %bitcast.60, bf16[512,4096]{1,0:T(8,128)(2,1)} %bitcast.66, ...), kind=kOutput, calls=%fused_computation.56 | convolution fusion | flops 2149842944 | bytes 19922948 | tf_op jit(solution)/shard_map/dot_general | solution.py:125
  (91 shorter events, 38.9 us)
Async XLA Ops:
  7.2 98.4 %copy-start = (f32[2048,8]{0,1:T(8,128)S(1)}, f32[2048,8]{0,1:T(8,128)}, u32[]{:S(2)}) copy-start(f32[2048,8]{0,1:T(8,128)} %param.13) | copy-start | bytes 196612
  7.2 95.0 %copy-start.15 = (s32[8]{0:T(128)S(1)}, s32[8]{0:T(128)}, u32[]{:S(2)}) copy-start(s32[8]{0:T(128)} %param.18) | copy-start | bytes 100
  7.2 97.4 %copy-start.13 = (s32[512,2]{0,1:T(2,128)S(1)}, s32[512,2]{0,1:T(2,128)}, u32[]{:S(2)}) copy-start(s32[512,2]{0,1:T(2,128)} %param.17) | copy-start | bytes 12292
  7.2 97.9 %copy-start.8 = (bf16[512,2048]{1,0:T(8,128)(2,1)S(1)}, bf16[512,2048]{1,0:T(8,128)(2,1)}, u32[]{:S(2)}) copy-start(bf16[512,2048]{1,0:T(8,128)(2,1)} %param.11) | copy-start | bytes 6291460
  7.2 98.4 %copy-start.14 = (f32[2048]{0:T(1024)S(1)}, f32[2048]{0:T(1024)}, u32[]{:S(2)}) copy-start(f32[2048]{0:T(1024)} %param.12) | copy-start | bytes 24580
  7.2 94.2 %all-gather.4.cloned.1.call-start = ((), (), s32[]{:S(2)}) async-start(), calls=%async_computation | async-start | bytes 18874368 | tf_op jit(solution)/shard_map/all_gather | solution.py:152
  8.0 168.1 %all-gather.6.cloned.1.call-start = ((), (), s32[]{:S(2)}) async-start(), calls=%async_computation.1 | async-start | bytes 4718592 | tf_op jit(solution)/shard_map/all_gather | solution.py:156
  101.5 133.6 %all-gather.8.cloned.1.call-start = ((), (), s32[]{:S(2)}) async-start(), calls=%async_computation.2 | async-start | bytes 18874368 | tf_op jit(solution)/shard_map/all_gather | solution.py:157
  144.7 31.4 %copy-start.9 = (bf16[512,2048]{1,0:T(8,128)(2,1)S(1)}, bf16[512,2048]{1,0:T(8,128)(2,1)}, u32[]{:S(2)}) copy-start(bf16[512,2048]{1,0:T(8,128)(2,1)} %param.11) | copy-start | bytes 6291460
  148.0 4.2 %copy-start.2 = (f32[4,512,1024]{2,1,0:T(8,128)}, f32[4,512,1024]{2,1,0:T(8,128)S(1)}, u32[]{:S(2)}) copy-start(f32[4,512,1024]{2,1,0:T(8,128)S(1)} %get-tuple-element.145) | copy-start | bytes 25165828 | tf_op jit(solution)/shard_map/while
  164.3 3.2 %copy-start.2 = (f32[4,512,1024]{2,1,0:T(8,128)}, f32[4,512,1024]{2,1,0:T(8,128)S(1)}, u32[]{:S(2)}) copy-start(f32[4,512,1024]{2,1,0:T(8,128)S(1)} %get-tuple-element.145) | copy-start | bytes 25165828 | tf_op jit(solution)/shard_map/while
  185.7 1.9 copy-start.11
  185.7 1.9 copy-start.12
  186.4 1.7 copy-start.5
  187.5 4.7 %copy-start.6 = (bf16[512,4,1,128]{3,2,1,0:T(2,128)(2,1)}, bf16[512,4,1,128]{3,2,1,0:T(2,128)(2,1)S(1)}, u32[]{:S(2)}) copy-start(bf16[512,4,1,128]{3,2,1,0:T(2,128)(2,1)S(1)} %slice.53) | copy-start | bytes 1572868
  190.0 2.2 copy-start.10
  235.1 11.0 %copy-start.3 = (bf16[8,512,2048]{2,1,0:T(8,128)(2,1)S(1)}, bf16[8,512,2048]{2,1,0:T(8,128)(2,1)}, u32[]{:S(2)}) copy-start(bf16[8,512,2048]{2,1,0:T(8,128)(2,1)} %all-gather.8.cloned.1.call-done) | copy-start | bytes 50331652
  235.1 12.2 %copy-start.4 = (bf16[64,8,8,512]{3,1,2,0:T(8,128)(2,1)S(1)}, bf16[64,8,8,512]{3,1,2,0:T(8,128)(2,1)}, u32[]{:S(2)}) copy-start(bf16[64,8,8,512]{3,1,2,0:T(8,128)(2,1)} %copy.50) | copy-start | bytes 12582916
  244.5 13.7 %collective-permute-start = (bf16[128,2048]{1,0:T(8,128)(2,1)}, bf16[128,2048]{1,0:T(8,128)(2,1)S(1)}, u32[]{:S(2)}, u32[]{:S(2)}) collective-permute-start(bf16[128,2048]{1,0:T(8,128)(2,1)} %convolution_convert_fusion.3), channel_id=1, source_target_pairs={{0,1},{1,2},{2,3},{3,0},{4,5},{5,6},{6,7},{7,4},{8,9},{9,10},{10,1... | collective-permute-start | bytes 1572872 | tf_op jit(solution)/shard_map/ppermute | solution.py:127
  250.7 5.7 %copy-start.7 = (bf16[512,4,1,128]{3,2,1,0:T(2,128)(2,1)S(1)}, bf16[512,4,1,128]{3,2,1,0:T(2,128)(2,1)}, u32[]{:S(2)}) copy-start(bf16[512,4,1,128]{3,2,1,0:T(2,128)(2,1)} %copy-done.6) | copy-start | bytes 1572868
  250.7 40.3 %collective-permute-start.1 = (bf16[128,2048]{1,0:T(8,128)(2,1)}, bf16[128,2048]{1,0:T(8,128)(2,1)}, u32[]{:S(2)}, u32[]{:S(2)}) collective-permute-start(bf16[128,2048]{1,0:T(8,128)(2,1)} %convolution_convert_fusion.2), channel_id=1, source_target_pairs={{0,2},{1,3},{2,0},{3,1},{4,6},{5,7},{6,4},{7,5},{8,10},{9,11},{10,... | collective-permute-start | bytes 1572872 | tf_op jit(solution)/shard_map/ppermute | solution.py:127
  256.1 37.4 %collective-permute-start.2 = (bf16[128,2048]{1,0:T(8,128)(2,1)}, bf16[128,2048]{1,0:T(8,128)(2,1)}, u32[]{:S(2)}, u32[]{:S(2)}) collective-permute-start(bf16[128,2048]{1,0:T(8,128)(2,1)} %convolution_convert_fusion.1), channel_id=1, source_target_pairs={{0,3},{1,0},{2,1},{3,2},{4,7},{5,4},{6,5},{7,6},{8,11},{9,8},{10,9... | collective-permute-start | bytes 1572872 | tf_op jit(solution)/shard_map/ppermute | solution.py:127
  293.4 9.5 %copy-start.1 = (f32[2048,8]{0,1:T(8,128)S(1)}, f32[2048,8]{0,1:T(8,128)}, u32[]{:S(2)}) copy-start(f32[2048,8]{0,1:T(8,128)} %param.13) | copy-start | bytes 196612
Sparse Core Ops, SparseCore 0:
  10.0 91.4 all-gather.3
  103.3 36.7 all-gather.5
  142.0 93.1 all-gather.7
where the time goes:
time: 313 us; the launch traced here: 310 us
  waiting for transfers between devices  150 us (48%)
  matrix products  73.2 us (23%)
  other arithmetic  36.2 us (12%)
  local copies, waits for them, and re-layouts  30.8 us (10%)
  between operations  15.1 us (5%)
  starting transfers between devices  3.91 us (1%)
    all_gather x1, waiting for transfers between devices, shards(): query_full = lax.all_gather(query_weight, 'req', axis=1, tiled=True)  93.4 us
    ppermute x3, waiting for transfers between devices, exchange_reduce(): lax.ppermute(part, axis, [(src, (src + shift) % count) for src in range(c...  35.6 us
    dot_general x4, matrix products, exchange_reduce(): jnp.dot(block_rows, weight, preferred_element_type=jnp.float32)  25.5 us
    dot_general x3, matrix products, absorb(): jnp.einsum('hqk,hkd->hqd', weights.astype(jnp.bfloat16), value_rows, pref...  21.5 us
    all_gather x1, waiting for transfers between devices, shards(): out_full = lax.all_gather(out_weight, 'req', axis=2, tiled=True)  20 us
    dot_general x1, matrix products, shards(): jnp.einsum('tc,ecn->ten', normed, query_full, preferred_element_type=jnp....  11.9 us
    reduce_sum x1, other arithmetic, shards(): jnp.sum(jnp.where(one_hot[..., None], query_all[:, None], 0.0), axis=2)  8.24 us
    reduce_sum x1, other arithmetic, shards(): jnp.sum(jnp.where(one_hot[..., None], weighted[:, :, None, :], 0), axis=1)  7.15 us
  transfers between devices with their start and end apart: 6, of which 5 were waited for; matrix products, arithmetic and copies ran while one was open for 38% of the time, Pallas kernels for 0%

commit v1 on v0

--- a/solution.py
+++ b/solution.py
@@ -149,7 +149,16 @@
     cache_len = kv_cache.shape[2]
     block_len = min(512, cache_len // 4)
     gate_values = gate_pair(normed, router_weight, expert_ids)
-    query_full = lax.all_gather(query_weight, "req", axis=1, tiled=True)
+    local_out, current_arr = (lax.axis_size("req"), lax.axis_index("req"))
+    query_full, lower = (query_weight, 1)
+    while lower < local_out:
+        back = lax.ppermute(
+            query_full, axis_name="req", perm=tuple(((at, at ^ lower) for at in range(local_out)))
+        )
+        w1 = jnp.concatenate([query_full, back], axis=1)
+        r1 = jnp.concatenate([back, query_full], axis=1)
+        query_full = jnp.where(current_arr & lower == 0, w1, r1)
+        lower = 2 * lower
     query_full, kv_weight, out_weight = lax.optimization_barrier(
         (query_full, kv_weight, out_weight)
     )

time: 313 us -> 535 us (1.71)
  waiting for transfers between devices: 150 us -> 333 us
  other arithmetic: 36.2 us -> 71.4 us
    ppermute x0 -> x3, waiting for transfers between devices: none -> 275 us  [shards(): lax.ppermute(query_full, axis_name='req', perm=tuple(((at, at ^ lower) fo...]
    all_gather x1 -> x0, waiting for transfers between devices: 93.4 us -> none  [shards(): query_full = lax.all_gather(query_weight, 'req', axis=1, tiled=True)]
    select_n x0 -> x3, other arithmetic: none -> 35.2 us  [shards(): query_full = jnp.where(current_arr & lower == 0, w1, r1)]
  transfers between devices with their start and end apart: 6 -> 8, of which waited for: 5 -> 7; matrix products, arithmetic and copies ran while one was open for 38% -> 22% of each run, Pallas kernels for 0% -> 0%
where the time goes in v1:
time: 535 us; the launch traced here: 530 us
  waiting for transfers between devices  333 us (62%)
  matrix products  73.5 us (14%)
  other arithmetic  71.4 us (13%)
  local copies, waits for them, and re-layouts  30.1 us (6%)
  between operations  15.4 us (3%)
  starting transfers between devices  7.05 us (1%)
    ppermute x3, waiting for transfers between devices, shards(): lax.ppermute(query_full, axis_name='req', perm=tuple(((at, at ^ lower) fo...  275 us
    ppermute x3, waiting for transfers between devices, exchange_reduce(): lax.ppermute(part, axis, [(src, (src + shift) % count) for src in range(c...  35.6 us
    select_n x3, other arithmetic, shards(): query_full = jnp.where(current_arr & lower == 0, w1, r1)  35.2 us
    dot_general x4, matrix products, exchange_reduce(): jnp.dot(block_rows, weight, preferred_element_type=jnp.float32)  25.5 us
    dot_general x3, matrix products, absorb(): jnp.einsum('hqk,hkd->hqd', weights.astype(jnp.bfloat16), value_rows, pref...  21.8 us
    all_gather x1, waiting for transfers between devices, shards(): out_full = lax.all_gather(out_weight, 'req', axis=2, tiled=True)  21.8 us
    dot_general x1, matrix products, shards(): jnp.einsum('tc,ecn->ten', normed, query_full, preferred_element_type=jnp....  11.9 us
  transfers between devices with their start and end apart: 8, of which 7 were waited for; matrix products, arithmetic and copies ran while one was open for 22% of the time, Pallas kernels for 0%

profile of v1, /device:TPU:9, one launch (start us, length us, event | category | flops | bytes accessed | tf_op | source)
XLA Modules:
  0.0 530.3 jit_solution(4950938877877679058)
XLA Ops:
  8.0 4.0 collective-permute-done
  12.0 4.8 maximum_select_fusion.2
  18.0 90.9 %collective-permute-done.1 = bf16[8,512,512]{2,1,0:T(8,128)(2,1)} collective-permute-done((bf16[8,512,512]{2,1,0:T(8,128)(2,1)}, bf16[8,512,512]{2,1,0:T(8,128)(2,1)}, u32[]{:S(2)}, u32[]{:S(2)}) %collective-permute-start.1) | collective-permute-done | bytes 4194336 | tf_op jit(solution)/shard_map/ppermute | solution.py:155
  108.9 10.9 %maximum_select_fusion.1 = bf16[8,1024,512]{2,1,0:T(8,128)(2,1)} fusion(bf16[8,512,512]{2,1,0:T(8,128)(2,1)} %collective-permute-done.1, bf16[8,512,512]{2,1,0:T(8,128)(2,1)} %maximum_select_fusion.2, pred[]{:T(512)S(6)} %eq.45), kind=kLoop, calls=%fused_computation.27 | loop fusion | flops 37748736 | bytes 16777216 | tf_op jit(solution)/shard_map/jit(_where)/select_n | solution.py:160
  121.0 179.8 %collective-permute-done.2 = bf16[8,1024,512]{2,1,0:T(8,128)(2,1)} collective-permute-done((bf16[8,1024,512]{2,1,0:T(8,128)(2,1)}, bf16[8,1024,512]{2,1,0:T(8,128)(2,1)}, u32[]{:S(2)}, u32[]{:S(2)}) %collective-permute-start.2) | collective-permute-done | bytes 8388640 | tf_op jit(solution)/shard_map/ppermute | solution.py:155
  300.8 19.6 %maximum_select_fusion = bf16[8,2048,512]{2,1,0:T(8,128)(2,1)} fusion(bf16[8,1024,512]{2,1,0:T(8,128)(2,1)} %collective-permute-done.2, bf16[8,1024,512]{2,1,0:T(8,128)(2,1)} %maximum_select_fusion.1, pred[]{:T(512)S(6)} %eq.44), kind=kLoop, calls=%fused_computation.25 | loop fusion | flops 75497472 | bytes 33554432 | tf_op jit(solution)/shard_map/jit(_where)/select_n | solution.py:160
  332.3 11.9 %fusion.31 = f32[512,8,512]{2,0,1:T(8,128)S(1)} fusion(bf16[8,2048,512]{2,1,0:T(8,128)(2,1)} %maximum_select_fusion, bf16[512,2048]{1,0:T(8,128)(2,1)S(1)} %copy-done.8, f32[2048]{0:T(1024)S(1)} %copy-done.14, f32[512]{0:T(512)S(1)} %add_rsqrt_fusion), kind=kOutput, calls=%fused_computation.47 | convolution fusion | flops 8594128896 | bytes 27273216 | tf_op jit(solution)/shard_map/tc,ecn->ten/dot_general | solution.py:168
  344.2 4.9 copy.40
  349.0 8.2 %select_reduce_fusion = f32[512,2,512]{2,1,0:T(2,128)} fusion(f32[512,8,512]{2,1,0:T(8,128)S(1)} %copy.40, pred[512,2,8]{2,1,0:T(4,128)(4,1)S(1)} %copy.38), kind=kLoop, calls=%fused_computation.26 | loop fusion | flops 7864320 | bytes 10493952 | tf_op jit(solution)/shard_map/reduce_sum | solution.py:177
  357.3 3.3 reshape.253
  363.6 31.3 %while.14 = (s32[]{:T(128)}, f32[4,1024]{1,0:T(4,128)S(1)}, f32[4,1024]{1,0:T(4,128)S(1)}, f32[4,1024,128]{2,1,0:T(8,128)}, s32[]{:T(128)}, /*index=5*/s32[]{:T(...) while((s32[]{:T(128)}, f32[4,1024]{1,0:T(4,128)S(1)}, ...), condition=%wide.region_7.8_spmd, body=%wide.region_4.7_spmd.sunk | while | flops 1102063616 | bytes 65276644 | solution.py:77
  370.7 9.3 %multiply_add_fusion.6 = f32[4,1024,128]{2,1,0:T(8,128)} fusion(f32[4,1024,128]{2,1,0:T(8,128)} %get-tuple-element.164, f32[4,512,1024]{2,1,0:T(8,128)} %copy-done.2, f32[4,1024]{1,0:T(4,128)S(1)} %max.8, pred[512]{0:T(512)(128)(4,1)S(1)} %fusion.81, f32[4,1024]{1,0:T(4,128)S(1)} %get-tuple-element.147, ...), kind=kOutput, calls=%fused_computation.10.clone.1 | convolution fusion | flops 548405248 | bytes 13141000 | tf_op jit(solution)/shard_map/while/body/hqk,hkd->hqd/dot_general | solution.py:58
  386.3 8.5 %multiply_add_fusion.6 = f32[4,1024,128]{2,1,0:T(8,128)} fusion(f32[4,1024,128]{2,1,0:T(8,128)} %get-tuple-element.164, f32[4,512,1024]{2,1,0:T(8,128)} %copy-done.2, f32[4,1024]{1,0:T(4,128)S(1)} %max.8, pred[512]{0:T(512)(128)(4,1)S(1)} %fusion.81, f32[4,1024]{1,0:T(4,128)S(1)} %get-tuple-element.147, ...), kind=kOutput, calls=%fused_computation.10.clone.1 | convolution fusion | flops 548405248 | bytes 13141000 | tf_op jit(solution)/shard_map/while/body/hqk,hkd->hqd/dot_general | solution.py:58
  394.9 5.9 %fusion.59 = f32[512,1024]{1,0:T(8,128)} fusion(bf16[2048,1024]{1,0:T(8,128)(2,1)} %all-gather.3.cloned.1.call-done, bf16[512,2048]{1,0:T(8,128)(2,1)S(1)} %copy-done.9, f32[2048]{0:T(1024)S(1)} %copy-done.14, f32[512]{0:T(512)S(1)} %add_rsqrt_fusion), kind=kOutput, calls=%fused_computation.104 | convolution fusion | flops 2151677952 | bytes 8398848 | tf_op jit(solution)/shard_map/dot_general | solution.py:167
  400.7 3.4 reshape.254
  410.7 4.0 divide_bitcast_fusion
  422.2 7.2 %select_reduce_fusion.1 = bf16[512,8,512]{2,1,0:T(8,128)(2,1)S(1)} fusion(pred[512,2,8]{2,1,0:T(4,128)(4,1)S(1)} %copy.38, bf16[512,2,512]{2,1,0:T(2,128)(2,1)S(1)} %multiply_convert_fusion), kind=kLoop, calls=%fused_computation.28 | loop fusion | flops 6291456 | bytes 5251072 | tf_op jit(solution)/shard_map/reduce_sum | solution.py:206
  429.4 4.2 copy.50
  433.6 21.8 %all-gather.5.cloned.1.call-done = bf16[8,512,2048]{2,1,0:T(8,128)(2,1)} async-done(((bf16[8,512,256]{2,1,0:T(8,128)(2,1)}), bf16[8,512,2048]{2,1,0:T(8,128)(2,1)}) %all-gather.5.cloned.1.call-update) | async-done | bytes 16777232 | tf_op jit(solution)/shard_map/all_gather | solution.py:166
  455.4 9.4 %convolution_convert_fusion.3 = bf16[128,2048]{1,0:T(8,128)(2,1)} fusion(bf16[4096,2048]{1,0:T(8,128)(2,1)} %bitcast.59, bf16[512,4096]{1,0:T(8,128)(2,1)} %bitcast.65, s32[]{:T(128)S(6)} %select_n.102), kind=kOutput, calls=%fused_computation.46 | convolution fusion | flops 2147745792 | bytes 18350084 | tf_op jit(solution)/shard_map/dot_general | solution.py:125
  467.6 3.3 convolution_convert_fusion.2
  473.0 3.3 convolution_convert_fusion.1
  478.4 32.8 %collective-permute-done.4 = bf16[128,2048]{1,0:T(8,128)(2,1)} collective-permute-done((bf16[128,2048]{1,0:T(8,128)(2,1)}, bf16[128,2048]{1,0:T(8,128)(2,1)}, u32[]{:S(2)}, u32[]{:S(2)}) %collective-permute-start.4) | collective-permute-done | bytes 524320 | tf_op jit(solution)/shard_map/ppermute | solution.py:127
  513.7 9.5 %add_convert_fusion.1 = bf16[128,2048]{1,0:T(8,128)(2,1)} fusion(bf16[128,2048]{1,0:T(8,128)(2,1)} %collective-permute-done.5, bf16[128,2048]{1,0:T(8,128)(2,1)} %collective-permute-done.4, bf16[128,2048]{1,0:T(8,128)(2,1)S(1)} %collective-permute-done.3, bf16[4096,2048]{1,0:T(8,128)(2,1)} %bitcast.60, bf16[512,4096]{1,0:T(8,128)(2,1)} %bitcast.66, ...), kind=kOutput, calls=%fused_computation.59 | convolution fusion | flops 2149842944 | bytes 19922948 | tf_op jit(solution)/shard_map/dot_general | solution.py:125
  (97 shorter events, 54.1 us)
Async XLA Ops:
  7.2 317.4 %copy-start = (f32[2048,8]{0,1:T(8,128)S(1)}, f32[2048,8]{0,1:T(8,128)}, u32[]{:S(2)}) copy-start(f32[2048,8]{0,1:T(8,128)} %param.13) | copy-start | bytes 196612
  7.2 387.7 %all-gather.3.cloned.1.call-start = ((), (), s32[]{:S(2)}) async-start(), calls=%async_computation | async-start | bytes 4718592 | tf_op jit(solution)/shard_map/all_gather | solution.py:165
  7.2 4.7 collective-permute-start
  16.8 92.1 %collective-permute-start.1 = (bf16[8,512,512]{2,1,0:T(8,128)(2,1)}, bf16[8,512,512]{2,1,0:T(8,128)(2,1)}, u32[]{:S(2)}, u32[]{:S(2)}) collective-permute-start(bf16[8,512,512]{2,1,0:T(8,128)(2,1)} %maximum_select_fusion.2), channel_id=1, source_target_pairs={{0,8},{4,12},{8,0},{12,4},{16,24},{20,28},{24,16},{28,20},{1,9},{5... | collective-permute-start | bytes 12582920 | tf_op jit(solution)/shard_map/ppermute | solution.py:155
  119.7 181.1 %collective-permute-start.2 = (bf16[8,1024,512]{2,1,0:T(8,128)(2,1)}, bf16[8,1024,512]{2,1,0:T(8,128)(2,1)}, u32[]{:S(2)}, u32[]{:S(2)}) collective-permute-start(bf16[8,1024,512]{2,1,0:T(8,128)(2,1)} %maximum_select_fusion.1), channel_id=1, source_target_pairs={{0,16},{4,20},{8,24},{12,28},{16,0},{20,4},{24,8},{28,12},{1,17},{... | collective-permute-start | bytes 25165832 | tf_op jit(solution)/shard_map/ppermute | solution.py:155
  121.0 200.2 %copy-start.15 = (s32[8]{0:T(128)S(1)}, s32[8]{0:T(128)}, u32[]{:S(2)}) copy-start(s32[8]{0:T(128)} %param.18) | copy-start | bytes 100
  121.0 201.6 %copy-start.13 = (s32[512,2]{0,1:T(2,128)S(1)}, s32[512,2]{0,1:T(2,128)}, u32[]{:S(2)}) copy-start(s32[512,2]{0,1:T(2,128)} %param.17) | copy-start | bytes 12292
  320.4 3.7 copy-start.8
  320.4 4.2 copy-start.14
  320.4 135.0 %all-gather.5.cloned.1.call-start = ((), (), s32[]{:S(2)}) async-start(), calls=%async_computation.1 | async-start | bytes 18874368 | tf_op jit(solution)/shard_map/all_gather | solution.py:166
  363.6 31.3 %copy-start.9 = (bf16[512,2048]{1,0:T(8,128)(2,1)S(1)}, bf16[512,2048]{1,0:T(8,128)(2,1)}, u32[]{:S(2)}) copy-start(bf16[512,2048]{1,0:T(8,128)(2,1)} %param.11) | copy-start | bytes 6291460
  366.9 3.8 copy-start.2
  383.1 3.2 copy-start.2
  404.2 1.9 copy-start.11
  404.2 1.9 copy-start.12
  406.0 4.7 copy-start.6
  408.5 2.2 copy-start.10
  455.4 11.0 %copy-start.3 = (bf16[8,512,2048]{2,1,0:T(8,128)(2,1)S(1)}, bf16[8,512,2048]{2,1,0:T(8,128)(2,1)}, u32[]{:S(2)}) copy-start(bf16[8,512,2048]{2,1,0:T(8,128)(2,1)} %all-gather.5.cloned.1.call-done) | copy-start | bytes 50331652
  455.4 12.2 %copy-start.4 = (bf16[64,8,8,512]{3,1,2,0:T(8,128)(2,1)S(1)}, bf16[64,8,8,512]{3,1,2,0:T(8,128)(2,1)}, u32[]{:S(2)}) copy-start(bf16[64,8,8,512]{3,1,2,0:T(8,128)(2,1)} %copy.50) | copy-start | bytes 12582916
  464.7 13.7 %collective-permute-start.3 = (bf16[128,2048]{1,0:T(8,128)(2,1)}, bf16[128,2048]{1,0:T(8,128)(2,1)S(1)}, u32[]{:S(2)}, u32[]{:S(2)}) collective-permute-start(bf16[128,2048]{1,0:T(8,128)(2,1)} %convolution_convert_fusion.3), channel_id=1, source_target_pairs={{0,1},{1,2},{2,3},{3,0},{4,5},{5,6},{6,7},{7,4},{8,9},{9,10},{10,1... | collective-permute-start | bytes 1572872 | tf_op jit(solution)/shard_map/ppermute | solution.py:127
  470.9 5.7 %copy-start.7 = (bf16[512,4,1,128]{3,2,1,0:T(2,128)(2,1)S(1)}, bf16[512,4,1,128]{3,2,1,0:T(2,128)(2,1)}, u32[]{:S(2)}) copy-start(bf16[512,4,1,128]{3,2,1,0:T(2,128)(2,1)} %copy-done.6) | copy-start | bytes 1572868
  470.9 40.3 %collective-permute-start.4 = (bf16[128,2048]{1,0:T(8,128)(2,1)}, bf16[128,2048]{1,0:T(8,128)(2,1)}, u32[]{:S(2)}, u32[]{:S(2)}) collective-permute-start(bf16[128,2048]{1,0:T(8,128)(2,1)} %convolution_convert_fusion.2), channel_id=1, source_target_pairs={{0,2},{1,3},{2,0},{3,1},{4,6},{5,7},{6,4},{7,5},{8,10},{9,11},{10,... | collective-permute-start | bytes 1572872 | tf_op jit(solution)/shard_map/ppermute | solution.py:127
  476.3 37.4 %collective-permute-start.5 = (bf16[128,2048]{1,0:T(8,128)(2,1)}, bf16[128,2048]{1,0:T(8,128)(2,1)}, u32[]{:S(2)}, u32[]{:S(2)}) collective-permute-start(bf16[128,2048]{1,0:T(8,128)(2,1)} %convolution_convert_fusion.1), channel_id=1, source_target_pairs={{0,3},{1,0},{2,1},{3,2},{4,7},{5,4},{6,5},{7,6},{8,11},{9,8},{10,9... | collective-permute-start | bytes 1572872 | tf_op jit(solution)/shard_map/ppermute | solution.py:127
  513.7 9.5 %copy-start.1 = (f32[2048,8]{0,1:T(8,128)S(1)}, f32[2048,8]{0,1:T(8,128)}, u32[]{:S(2)}) copy-start(f32[2048,8]{0,1:T(8,128)} %param.13) | copy-start | bytes 196612
  (1 other events, 1.7 us)
Sparse Core Ops, SparseCore 0:
  320.5 39.7 all-gather.2
  362.2 93.1 all-gather.4
